TPU v7x, 128 devices: a whole 4x4x4 slice. The times are simulated.
128 devices in a mesh: tok: 16 (over y, z), own: 8 (over x, core).
Axes of the slice: x: 4, y: 4, z: 4, core: 2. Of those that a mesh axis runs over, the one named last changes fastest.
Arguments:
- tokens: bfloat16 [16384, 1152], P(('tok', 'own')), may hold values from -6 to 6
- norm_gain: bfloat16 [1152], replicated, may hold values from 0.099609375 to 1.8984375
- w_query: bfloat16 [1152, 1152], replicated, as said below
- w_key: bfloat16 [1152, 384], replicated, as said below
- w_value: bfloat16 [1152, 384], replicated, may hold values from -0.1875 to 0.1875
- w_output: bfloat16 [1152, 1152], replicated, may hold values from -0.1875 to 0.1875
- qkv_in: bfloat16 [64, 48, 1152], P('own', None, 'tok'), may hold values from -0.1875 to 0.1875
- q_out: bfloat16 [64, 16, 1152], P('own', None, 'tok'), may hold values from -1.5 to 1.5
- kv_out: bfloat16 [64, 32, 384], P('own', None, 'tok'), may hold values from -1.5 to 1.5
- o_in: bfloat16 [64, 16, 1152], P('own', None, 'tok'), may hold values from -0.1875 to 0.1875
- o_out: bfloat16 [64, 16, 1152], P('own', None, 'tok'), may hold values from -1.5 to 1.5
- lengths: int32 [64], replicated, may hold values from 32 to 1536, as said below
- prompt_adapter: int32 [64], replicated, may hold values from 0 to 63
- adapter_slot: int32 [64], replicated, may hold values from 0 to 63, each once
Outputs:
- mixed: bfloat16 [16384, 1152], P(('tok', 'own'))
- kv_cache: bfloat16 [16384, 768], P(('tok', 'own'))
Inputs may be any that keep to these rules, and one draw needn't show every extreme that they name: `w_query`: entries lie within 6 / sqrt(1152) of zero. `w_key`: entries lie within 6 / sqrt(1152) of zero. `lengths`: lengths sum to 16384; exactly 8 prompts are 1536 long; the others hold 32 to 128 tokens, and one of them exactly 32. `adapter_slot`: each slot appears once; slot s is row s of the adapter tables, held by own index s // 8.
All inputs are finite; a program needn't handle non-finite values.
Results may differ from a plain program's by a relative error of at most 0.02.
Values may be sent and summed in bfloat16 or wider, within the bound.
No kernel may reach another device: no remote copies, remote signals or barrier semaphores. Data moves between devices by JAX's collectives and lax.ppermute only.
A program may use at most 128 MiB of HBM per device.

v0:
```python
import math
import jax
import jax.numpy as jnp
from jax import lax
from jax.sharding import PartitionSpec as P

D = 1152
HEADS = 18
KV_HEADS = 6
HEAD_WIDTH = 64
RANK = 16
REACH = 12
KVW = 384
SEG_DEV = 5
EPS = 1e-05
THETA = 10000.0


def from_behind(block, axis, distance):
    devices = range(lax.axis_size(axis))
    route = [(i - distance, i) for i in devices if i - distance in devices]
    return lax.ppermute(block, axis, route)


def rms_norm(row_block, gain_vec):
    widened = row_block.astype(jnp.float32)
    inverse_rms = lax.rsqrt(jnp.mean(widened * widened, axis=-1, keepdims=True) + EPS)
    return (widened * inverse_rms * gain_vec.astype(jnp.float32)).astype(jnp.bfloat16)


def prompt_index(positions, lengths):
    prompt_ends = jnp.cumsum(lengths)
    prompt_starts = prompt_ends - lengths
    inside = (positions[:, None] >= prompt_starts[None, :]).astype(jnp.int32)
    segment = jnp.sum(inside, axis=1) - 1
    members = jnp.arange(lengths.shape[0], dtype=jnp.int32)[None, :] == segment[:, None]
    offset = positions - jnp.sum(jnp.where(members, prompt_starts[None, :], 0), axis=1)
    return (segment, offset, members)


def slot_lookup(adapter, adapter_slot):
    matches = jnp.arange(adapter_slot.shape[0], dtype=jnp.int32)[None, :] == adapter[:, None]
    return jnp.sum(jnp.where(matches, adapter_slot[None, :], 0), axis=1)


def rotate(vectors, offset):
    half_dim = vectors.shape[-1] // 2
    frequency = jnp.exp(
        jnp.arange(half_dim, dtype=jnp.float32) * (-2.0 * math.log(THETA) / vectors.shape[-1])
    )
    angles = offset.astype(jnp.float32)[:, None] * frequency[None, :]
    cosine = jnp.cos(angles)[:, None, :]
    sine_table = jnp.sin(angles)[:, None, :]
    first_half = vectors[..., :half_dim]
    second_half = vectors[..., half_dim:]
    return jnp.concatenate(
        [
            first_half * cosine - second_half * sine_table,
            second_half * cosine + first_half * sine_table,
        ],
        axis=-1,
    )


def adapter_terms(row_block, code_rows, a_in, pieces):
    table_count, rank_cols, in_width = a_in.shape
    projected = lax.dot_general(
        row_block,
        a_in.reshape(table_count * rank_cols, in_width),
        (((1,), (1,)), ((), ())),
        preferred_element_type=jnp.float32,
    )
    chosen = (jnp.arange(table_count, dtype=jnp.int32)[None, :] == code_rows[:, None]).astype(
        jnp.float32
    )
    low_rank = (projected.reshape(-1, table_count, rank_cols) * chosen[:, :, None]).astype(
        jnp.bfloat16
    )
    results = []
    for col_start, b_table in pieces:
        width_rank = b_table.shape[1]
        section = low_rank[:, :, col_start : col_start + width_rank].reshape(
            -1, table_count * width_rank
        )
        results.append(
            jnp.dot(
                section,
                b_table.reshape(table_count * width_rank, b_table.shape[2]),
                preferred_element_type=jnp.float32,
            ).astype(jnp.bfloat16)
        )
    return tuple(results)


def on_device(
    tokens,
    norm_gain,
    w_query,
    w_key,
    w_value,
    w_output,
    qkv_in,
    q_out,
    kv_out,
    o_in,
    o_out,
    lengths,
    prompt_adapter,
    adapter_slot,
):
    tok_rows = tokens.shape[0]
    tok_count = lax.axis_size("tok")
    own_count = lax.axis_size("own")
    per_owner = qkv_in.shape[0]
    device_here = lax.axis_index(("tok", "own"))
    positions = device_here * tok_rows + jnp.arange(tok_rows, dtype=jnp.int32)
    segment, offset, members = prompt_index(positions, lengths)
    prompt_count = lengths.shape[0]
    first_segment = segment[0]
    code_rows = segment - first_segment
    normed = rms_norm(tokens, norm_gain)
    tables = (qkv_in, q_out, kv_out, o_in, o_out)
    table_shapes = tuple((table.shape[1:] for table in tables))
    packed = jnp.concatenate([table.reshape(per_owner, -1) for table in tables], axis=1)
    all_slots = lax.all_gather(packed, "own", axis=0, tiled=True)
    own_here = lax.axis_index("own")
    group_blocks = jnp.arange(tok_count, dtype=jnp.int32) * own_count + own_here
    prompt_starts = jnp.cumsum(lengths) - lengths
    group_first = (
        jnp.sum(
            (group_blocks[:, None] * tok_rows >= prompt_starts[None, :]).astype(jnp.int32), axis=1
        )
        - 1
    )
    group_segments = jnp.minimum(
        group_first[:, None] + jnp.arange(SEG_DEV, dtype=jnp.int32)[None, :], prompt_count - 1
    )
    group_slots = jnp.take(adapter_slot, jnp.take(prompt_adapter, group_segments))
    outgoing = jnp.take(all_slots, group_slots.reshape(-1), axis=0).reshape(
        tok_count, SEG_DEV, packed.shape[1]
    )
    incoming = lax.all_to_all(outgoing, "tok", 0, 0, tiled=True)
    selected = []
    col = 0
    for table_shape in table_shapes:
        width = table_shape[0] * table_shape[1]
        piece = incoming[:, :, col : col + width].reshape(
            tok_count, SEG_DEV, table_shape[0], table_shape[1]
        )
        col += width
        selected.append(
            jnp.transpose(piece, (1, 2, 0, 3)).reshape(
                SEG_DEV, table_shape[0], tok_count * table_shape[1]
            )
        )
    input_maps, query_maps, keyvalue_maps, output_in_maps, output_out_maps = selected
    delta_q, delta_k, delta_v = adapter_terms(
        normed,
        code_rows,
        input_maps,
        ((0, query_maps), (RANK, keyvalue_maps[:, :RANK]), (2 * RANK, keyvalue_maps[:, RANK:])),
    )
    base_q = jnp.dot(normed, w_query, preferred_element_type=jnp.float32)
    base_k = jnp.dot(normed, w_key, preferred_element_type=jnp.float32)
    base_v = jnp.dot(normed, w_value, preferred_element_type=jnp.float32)
    query_lin = (base_q + delta_q.astype(jnp.float32)).reshape(tok_rows, HEADS, HEAD_WIDTH)
    queries = rotate(query_lin, offset).reshape(tok_rows, D).astype(jnp.bfloat16)
    key_lin = (base_k + delta_k.astype(jnp.float32)).reshape(tok_rows, KV_HEADS, HEAD_WIDTH)
    key_rows = rotate(key_lin, offset).reshape(tok_rows, KVW).astype(jnp.bfloat16)
    value_rows = (base_v + delta_v.astype(jnp.float32)).astype(jnp.bfloat16)
    key_value = jnp.concatenate([key_rows, value_rows], axis=1)
    key_store = jnp.zeros(((REACH + 1) * tok_rows, 2 * KVW), jnp.bfloat16)
    key_store = lax.dynamic_update_slice_in_dim(key_store, key_value, REACH * tok_rows, 0)
    window = key_store
    moving = key_value
    for turn_index in range(REACH):
        moving = from_behind(moving, ("tok", "own"), 1)
        window = lax.dynamic_update_slice_in_dim(
            window, moving, (REACH - 1 - turn_index) * tok_rows, 0
        )
    key_positions = (
        device_here * tok_rows
        - REACH * tok_rows
        + jnp.arange((REACH + 1) * tok_rows, dtype=jnp.int32)
    )
    key_segment = prompt_index(key_positions, lengths)[0]
    allowed = (segment[:, None] == key_segment[None, :]) & (
        key_positions[None, :] <= positions[:, None]
    )
    groups = HEADS // KV_HEADS
    key_count = window.shape[0]
    query_head_rows = queries.reshape(tok_rows, KV_HEADS, groups, HEAD_WIDTH)
    key_head_rows = window[:, :KVW].reshape(key_count, KV_HEADS, HEAD_WIDTH)
    value_head_rows = window[:, KVW:].reshape(key_count, KV_HEADS, HEAD_WIDTH)
    score_matrix = jnp.einsum(
        "qkzr,ckr->kzqc", query_head_rows, key_head_rows, preferred_element_type=jnp.float32
    ) * HEAD_WIDTH ** (-0.5)
    score_matrix = jnp.where(allowed[None, None], score_matrix, -1e30)
    top_score = jnp.max(score_matrix, axis=-1, keepdims=True)
    exp_scores = jnp.exp(score_matrix - top_score)
    row_total = jnp.sum(exp_scores, axis=-1)
    rounded_values = exp_scores.astype(jnp.bfloat16)
    summed_rows = jnp.einsum(
        "iyxv,vip->xiyp", rounded_values, value_head_rows, preferred_element_type=jnp.float32
    )
    attn_rows = (
        (summed_rows / jnp.transpose(row_total, (2, 0, 1))[..., None])
        .reshape(tok_rows, D)
        .astype(jnp.bfloat16)
    )
    delta_o = adapter_terms(attn_rows, code_rows, output_in_maps, ((0, output_out_maps),))[0]
    projected_out = jnp.dot(
        attn_rows, w_output, preferred_element_type=jnp.float32
    ) + delta_o.astype(jnp.float32)
    mixed_rows = (tokens.astype(jnp.float32) + projected_out).astype(jnp.bfloat16)
    return (mixed_rows, key_value)


def solution(mesh):
    return jax.shard_map(
        on_device,
        mesh=mesh,
        in_specs=(
            P(("tok", "own"), None),
            P(),
            P(),
            P(),
            P(),
            P(),
            P("own", None, "tok"),
            P("own", None, "tok"),
            P("own", None, "tok"),
            P("own", None, "tok"),
            P("own", None, "tok"),
            P(),
            P(),
            P(),
        ),
        out_specs=(P(("tok", "own"), None), P(("tok", "own"), None)),
        check_vma=False,
    )
```

profile of v0, /device:TPU:24, one launch (start us, length us, event | category | flops | bytes accessed | tf_op | source)
XLA Modules:
  0.0 273.8 jit_solution(17576496565474559692)
XLA Ops:
  9.0 15.0 %all_gather.3 = bf16[64,7680]{1,0:T(8,128)(2,1)} all-gather(bf16[8,7680]{1,0:T(8,128)(2,1)S(1)} %constant_dynamic-update-slice_fusion), channel_id=1, replica_groups=mesh['tok'=16,'own'=8] {'own'}, dimensions={0}, use_global_device_ids=true | all-gather | bytes 1105920 | tf_op jit(solution)/shard_map/all_gather | solution.py:125
  24.0 4.8 %gather_fusion = bf16[80,7680]{1,0:T(8,128)(2,1)} fusion(bf16[64,7680]{1,0:T(8,128)(2,1)} %all_gather.3, s32[1024]{0:T(1024)S(1)} %pad_clamp_fusion), kind=kCustom, calls=%fused_computation.2 | custom fusion | bytes 2457920 | tf_op jit(solution)/shard_map/jit(_take)/gather | solution.py:139
  28.8 2.6 gather.10
  31.5 3.1 %broadcast_select_fusion = bf16[16,5,7680]{2,1,0:T(8,128)(2,1)} fusion(bf16[16,5,7680]{2,1,0:T(8,128)(2,1)} %gather.10, pred[16,5]{1,0:T(8,128)(4,1)S(1)} %get-tuple-element.3), kind=kLoop, calls=%fused_computation.18 | loop fusion | flops 614400 | bytes 2457680 | tf_op jit(solution)/shard_map/jit(_take)/select_n | solution.py:139
  34.6 8.3 %all-to-all-start = ((bf16[16,5,7680]{2,1,0:T(8,128)(2,1)}), bf16[16,5,7680]{2,1,0:T(8,128)(2,1)}, u32[]{:S(2)}, u32[]{:S(2)}) async-start(bf16[16,5,7680]{2,1,0:T(8,128)(2,1)} %broadcast_select_fusion), calls=%async_computation | async-start | bytes 3932160 | tf_op jit(solution)/shard_map/all_to_all | solution.py:142
  44.9 25.3 %all-to-all-done = bf16[16,5,7680]{2,1,0:T(8,128)(2,1)} async-done(((bf16[16,5,7680]{2,1,0:T(8,128)(2,1)}), bf16[16,5,7680]{2,1,0:T(8,128)(2,1)}, u32[]{:S(2)}, u32[]{:S(2)}) %all-to-all-start) | async-done | bytes 1228832 | tf_op jit(solution)/shard_map/all_to_all | solution.py:142
  71.2 1.9 reshape.334
  73.0 2.2 copy.47
  75.2 2.3 reshape.335
  78.9 2.7 reshape.333
  81.5 2.4 copy.45
  84.0 2.2 dot_general.41
  93.0 1.9 collective-permute-start
  95.0 9.3 %collective-permute-done = bf16[128,768]{1,0:T(8,128)(2,1)S(1)} collective-permute-done((bf16[128,768]{1,0:T(8,128)(2,1)S(1)}, bf16[128,768]{1,0:T(8,128)(2,1)S(1)}, u32[]{:S(2)}, u32[]{:S(2)}) %collective-permute-start) | collective-permute-done | bytes 196640 | tf_op jit(solution)/shard_map/ppermute | solution.py:22
  104.2 2.1 collective-permute-start.1
  107.4 8.1 %collective-permute-done.1 = bf16[128,768]{1,0:T(8,128)(2,1)} collective-permute-done((bf16[128,768]{1,0:T(8,128)(2,1)S(1)}, bf16[128,768]{1,0:T(8,128)(2,1)}, u32[]{:S(2)}, u32[]{:S(2)}) %collective-permute-start.1) | collective-permute-done | bytes 196640 | tf_op jit(solution)/shard_map/ppermute | solution.py:22
  115.5 1.9 collective-permute-start.2
  117.5 2.0 fusion.43
  123.8 2.0 reshape_reshape.9
  125.8 1.7 copy.56
  129.8 2.0 dot_general.51
  131.7 1.7 copy.52
  137.0 1.9 collective-permute-start.3
  139.9 8.5 %collective-permute-done.3 = bf16[128,768]{1,0:T(8,128)(2,1)S(1)} collective-permute-done((bf16[128,768]{1,0:T(8,128)(2,1)}, bf16[128,768]{1,0:T(8,128)(2,1)S(1)}, u32[]{:S(2)}, u32[]{:S(2)}) %collective-permute-start.3) | collective-permute-done | bytes 196640 | tf_op jit(solution)/shard_map/ppermute | solution.py:22
  148.4 1.9 collective-permute-start.4
  150.3 2.2 convolution_add_fusion.1
  152.5 2.1 copy.54
  154.9 4.8 %collective-permute-done.4 = bf16[128,768]{1,0:T(8,128)(2,1)} collective-permute-done((bf16[128,768]{1,0:T(8,128)(2,1)S(1)}, bf16[128,768]{1,0:T(8,128)(2,1)}, u32[]{:S(2)}, u32[]{:S(2)}) %collective-permute-start.4) | collective-permute-done | bytes 196640 | tf_op jit(solution)/shard_map/ppermute | solution.py:22
  159.7 1.9 collective-permute-start.5
  161.8 9.4 %collective-permute-done.5 = bf16[128,768]{1,0:T(8,128)(2,1)S(1)} collective-permute-done((bf16[128,768]{1,0:T(8,128)(2,1)}, bf16[128,768]{1,0:T(8,128)(2,1)S(1)}, u32[]{:S(2)}, u32[]{:S(2)}) %collective-permute-start.5) | collective-permute-done | bytes 196640 | tf_op jit(solution)/shard_map/ppermute | solution.py:22
  171.1 1.9 collective-permute-start.6
  173.1 9.2 %collective-permute-done.6 = bf16[128,768]{1,0:T(8,128)(2,1)S(1)} collective-permute-done((bf16[128,768]{1,0:T(8,128)(2,1)S(1)}, bf16[128,768]{1,0:T(8,128)(2,1)S(1)}, u32[]{:S(2)}, u32[]{:S(2)}) %collective-permute-start.6) | collective-permute-done | bytes 196640 | tf_op jit(solution)/shard_map/ppermute | solution.py:22
  182.3 1.9 collective-permute-start.7
  186.1 7.4 %collective-permute-done.7 = bf16[128,768]{1,0:T(8,128)(2,1)S(1)} collective-permute-done((bf16[128,768]{1,0:T(8,128)(2,1)S(1)}, bf16[128,768]{1,0:T(8,128)(2,1)S(1)}, u32[]{:S(2)}, u32[]{:S(2)}) %collective-permute-start.7) | collective-permute-done | bytes 196640 | tf_op jit(solution)/shard_map/ppermute | solution.py:22
  193.5 1.9 collective-permute-start.8
  196.4 8.3 %collective-permute-done.8 = bf16[128,768]{1,0:T(8,128)(2,1)S(1)} collective-permute-done((bf16[128,768]{1,0:T(8,128)(2,1)S(1)}, bf16[128,768]{1,0:T(8,128)(2,1)S(1)}, u32[]{:S(2)}, u32[]{:S(2)}) %collective-permute-start.8) | collective-permute-done | bytes 196640 | tf_op jit(solution)/shard_map/ppermute | solution.py:22
  204.7 1.9 collective-permute-start.9
  206.7 9.2 %collective-permute-done.9 = bf16[128,768]{1,0:T(8,128)(2,1)S(1)} collective-permute-done((bf16[128,768]{1,0:T(8,128)(2,1)S(1)}, bf16[128,768]{1,0:T(8,128)(2,1)S(1)}, u32[]{:S(2)}, u32[]{:S(2)}) %collective-permute-start.9) | collective-permute-done | bytes 196640 | tf_op jit(solution)/shard_map/ppermute | solution.py:22
  215.9 1.9 collective-permute-start.10
  217.9 9.2 %collective-permute-done.10 = bf16[128,768]{1,0:T(8,128)(2,1)S(1)} collective-permute-done((bf16[128,768]{1,0:T(8,128)(2,1)S(1)}, bf16[128,768]{1,0:T(8,128)(2,1)S(1)}, u32[]{:S(2)}, u32[]{:S(2)}) %collective-permute-start.10) | collective-permute-done | bytes 196640 | tf_op jit(solution)/shard_map/ppermute | solution.py:22
  227.1 1.9 collective-permute-start.11
  229.1 9.2 %collective-permute-done.11 = bf16[128,768]{1,0:T(8,128)(2,1)S(1)} collective-permute-done((bf16[128,768]{1,0:T(8,128)(2,1)S(1)}, bf16[128,768]{1,0:T(8,128)(2,1)S(1)}, u32[]{:S(2)}, u32[]{:S(2)}) %collective-permute-start.11) | collective-permute-done | bytes 196640 | tf_op jit(solution)/shard_map/ppermute | solution.py:22
  238.3 1.7 fusion.42
  240.1 2.5 copy.51
  242.6 2.5 copy.50
  245.1 9.0 %fusion.2 = (f32[6,3,128]{2,1,0:T(4,128)S(1)}, f32[6,1664,128,3]{2,1,3,0:T(8,128)}) fusion(pred[128,1664]{0,1:T(8,128)(4,1)S(1)} %compare_and_fusion, bf16[1664,6,64,1]{0,2,3,1:T(8,128)(2,1)} %bitcast.101, bf16[128,6,3,64]{0,3,2,1:T(8,128)(2,1)S(1)} %bitcast.105), kind=kOutput, calls=%fused_computation.7 | convolution fusion | flops 502232832 | bytes 17130496 | tf_op jit(solution)/shard_map/qkzr,ckr->kzqc/dot_general | solution.py:195
  254.0 8.6 %fusion = f32[6,3,128]{2,1,0:T(4,128)S(1)} fusion(f32[6,1664,128,3]{2,1,3,0:T(8,128)} %get-tuple-element.17, f32[6,3,128]{2,1,0:T(4,128)S(1)} %get-tuple-element.16, pred[128,1664]{0,1:T(8,128)(4,1)S(1)} %compare_and_fusion), kind=kLoop, calls=%fused_computation.5 | loop fusion | flops 15333120 | bytes 15566848 | tf_op jit(solution)/shard_map/reduce_sum | solution.py:201
  262.7 9.2 %fusion.23 = bf16[128,6,3,64]{0,3,2,1:T(8,128)(2,1)S(1)} fusion(bf16[1664,6,64,1]{0,2,3,1:T(8,128)(2,1)S(1)} %bitcast.109, f32[6,1664,128,3]{2,1,3,0:T(8,128)} %get-tuple-element.17, f32[6,3,128]{2,1,0:T(4,128)S(1)} %get-tuple-element.16, pred[128,1664]{0,1:T(8,128)(4,1)S(1)} %compare_and_fusion, f32[128,6,3]{0,2,1:T(4,128)S(1)} %bitcast.116), kind=kOutput, calls=%fused_computation.34 | convolution fusion | flops 506363904 | bytes 17139712 | tf_op jit(solution)/shard_map/iyxv,vip->xiyp/dot_general | solution.py:203
  (157 shorter events, 36.4 us)
Async XLA Ops:
  0.6 149.7 %copy-start = (bf16[1152,1152]{1,0:T(8,128)(2,1)S(1)}, bf16[1152,1152]{1,0:T(8,128)(2,1)}, u32[]{:S(2)}) copy-start(bf16[1152,1152]{1,0:T(8,128)(2,1)} %param.18) | copy-start | bytes 7962628
  0.6 4.8 %copy-start.1 = (s32[64]{0:T(128)S(1)}, s32[64]{0:T(128)}, u32[]{:S(2)}) copy-start(s32[64]{0:T(128)} %param.28) | copy-start | bytes 772
  5.4 1.5 copy-start.2
  7.0 1.6 copy-start.19
  7.0 1.7 copy-start.23
  34.6 8.3 %copy-start.3 = (bf16[128,1152]{1,0:T(8,128)(2,1)S(1)}, bf16[128,1152]{1,0:T(8,128)(2,1)}, u32[]{:S(2)}) copy-start(bf16[128,1152]{1,0:T(8,128)(2,1)} %param.16) | copy-start | bytes 884740
  34.6 9.4 %copy-start.26 = (bf16[1152]{0:T(1024)(128)(2,1)S(1)}, bf16[1152]{0:T(1024)(128)(2,1)}, u32[]{:S(2)}) copy-start(bf16[1152]{0:T(1024)(128)(2,1)} %param.17) | copy-start | bytes 6916
  34.6 35.6 %all-to-all-start = ((bf16[16,5,7680]{2,1,0:T(8,128)(2,1)}), bf16[16,5,7680]{2,1,0:T(8,128)(2,1)}, u32[]{:S(2)}, u32[]{:S(2)}) async-start(bf16[16,5,7680]{2,1,0:T(8,128)(2,1)} %broadcast_select_fusion), calls=%async_computation | async-start | bytes 3932160 | tf_op jit(solution)/shard_map/all_to_all | solution.py:142
  42.9 27.3 %copy-start.29 = (s32[128]{0:T(128)}, s32[128]{0:T(128)S(1)}, u32[]{:S(2)}) copy-start(s32[128]{0:T(128)S(1)} %iota_add_fusion.1) | copy-start | bytes 1540
  43.1 1.0 copy-start.20
  43.2 27.0 %copy-start.31 = (s32[128]{0:T(128)}, s32[128]{0:T(128)S(1)}, u32[]{:S(2)}) copy-start(s32[128]{0:T(128)S(1)} %broadcast_add_fusion.1) | copy-start | bytes 1540
  44.0 42.1 %copy-start.18 = (f32[1152]{0:T(1024)}, f32[1152]{0:T(1024)S(1)}, u32[]{:S(2)}) copy-start(f32[1152]{0:T(1024)S(1)} %convert_element_type.91) | copy-start | bytes 13828
  44.1 42.1 %copy-start.25 = (f32[128]{0:T(128)}, f32[128]{0:T(128)S(1)}, u32[]{:S(2)}) copy-start(f32[128]{0:T(128)S(1)} %add_rsqrt_fusion) | copy-start | bytes 1540
  44.1 42.0 %copy-start.27 = (f32[128,5]{0,1:T(8,128)}, f32[128,5]{0,1:T(8,128)S(1)}, u32[]{:S(2)}) copy-start(f32[128,5]{0,1:T(8,128)S(1)} %fusion.34) | copy-start | bytes 7684
  44.9 45.6 %copy-start.15 = (f32[128,32]{0,1:T(8,128)}, f32[128,32]{0,1:T(8,128)S(1)}, u32[]{:S(2)}) copy-start(f32[128,32]{0,1:T(8,128)S(1)} %get-tuple-element.14) | copy-start | bytes 49156
  86.6 2.1 copy-start.22
  90.5 4.5 %copy-start.24 = (s32[1664]{0:T(1024)S(1)}, s32[1664]{0:T(1024)}, u32[]{:S(2)}) copy-start(s32[1664]{0:T(1024)} %convert_reduce_fusion) | copy-start | bytes 19972
  90.5 15.9 %copy-start.21 = (s32[1664]{0:T(1024)S(1)}, s32[1664]{0:T(1024)}, u32[]{:S(2)}) copy-start(s32[1664]{0:T(1024)} %copy-done.20) | copy-start | bytes 19972
  90.5 15.9 %copy-start.30 = (s32[128]{0:T(128)S(1)}, s32[128]{0:T(128)}, u32[]{:S(2)}) copy-start(s32[128]{0:T(128)} %copy-done.29) | copy-start | bytes 1540
  90.5 15.9 %copy-start.32 = (s32[128]{0:T(128)S(1)}, s32[128]{0:T(128)}, u32[]{:S(2)}) copy-start(s32[128]{0:T(128)} %copy-done.31) | copy-start | bytes 1540
  93.0 22.5 %copy-start.7 = (bf16[128,768]{1,0:T(8,128)(2,1)}, bf16[128,768]{1,0:T(8,128)(2,1)S(1)}, u32[]{:S(2)}) copy-start(bf16[128,768]{1,0:T(8,128)(2,1)S(1)} %pad_maximum_fusion.1) | copy-start | bytes 589828
  93.0 11.2 %collective-permute-start = (bf16[128,768]{1,0:T(8,128)(2,1)S(1)}, bf16[128,768]{1,0:T(8,128)(2,1)S(1)}, u32[]{:S(2)}, u32[]{:S(2)}) collective-permute-start(bf16[128,768]{1,0:T(8,128)(2,1)S(1)} %pad_maximum_fusion.1), channel_id=1, source_target_pairs={{0,1},{1,2},{2,3},{3,4},{4,5},{5,6},{6,7},{7,8},{8,9},{9,10},{10,1... | collective-permute-start | bytes 589832 | tf_op jit(solution)/shard_map/ppermute | solution.py:22
  104.2 11.3 %copy-start.10 = (bf16[128,768]{1,0:T(8,128)(2,1)}, bf16[128,768]{1,0:T(8,128)(2,1)S(1)}, u32[]{:S(2)}) copy-start(bf16[128,768]{1,0:T(8,128)(2,1)S(1)} %collective-permute-done) | copy-start | bytes 589828
  104.2 11.3 %collective-permute-start.1 = (bf16[128,768]{1,0:T(8,128)(2,1)S(1)}, bf16[128,768]{1,0:T(8,128)(2,1)}, u32[]{:S(2)}, u32[]{:S(2)}) collective-permute-start(bf16[128,768]{1,0:T(8,128)(2,1)S(1)} %collective-permute-done), channel_id=1, source_target_pairs={{0,1},{1,2},{2,3},{3,4},{4,5},{5,6},{6,7},{7,8},{8,9},{9,10},{10,1... | collective-permute-start | bytes 589832 | tf_op jit(solution)/shard_map/ppermute | solution.py:22
  115.5 21.4 %collective-permute-start.2 = (bf16[128,768]{1,0:T(8,128)(2,1)}, bf16[128,768]{1,0:T(8,128)(2,1)}, u32[]{:S(2)}, u32[]{:S(2)}) collective-permute-start(bf16[128,768]{1,0:T(8,128)(2,1)} %collective-permute-done.1), channel_id=1, source_target_pairs={{0,1},{1,2},{2,3},{3,4},{4,5},{5,6},{6,7},{7,8},{8,9},{9,10},{10,1... | collective-permute-start | bytes 589832 | tf_op jit(solution)/shard_map/ppermute | solution.py:22
  137.0 11.4 %collective-permute-start.3 = (bf16[128,768]{1,0:T(8,128)(2,1)}, bf16[128,768]{1,0:T(8,128)(2,1)S(1)}, u32[]{:S(2)}, u32[]{:S(2)}) collective-permute-start(bf16[128,768]{1,0:T(8,128)(2,1)} %collective-permute-done.2), channel_id=1, source_target_pairs={{0,1},{1,2},{2,3},{3,4},{4,5},{5,6},{6,7},{7,8},{8,9},{9,10},{10,1... | collective-permute-start | bytes 589832 | tf_op jit(solution)/shard_map/ppermute | solution.py:22
  139.9 14.8 %copy-start.8 = (bf16[128,768]{1,0:T(8,128)(2,1)S(1)}, bf16[128,768]{1,0:T(8,128)(2,1)}, u32[]{:S(2)}) copy-start(bf16[128,768]{1,0:T(8,128)(2,1)} %copy-done.7) | copy-start | bytes 589828
  148.4 6.2 %copy-start.12 = (bf16[128,768]{1,0:T(8,128)(2,1)}, bf16[128,768]{1,0:T(8,128)(2,1)S(1)}, u32[]{:S(2)}) copy-start(bf16[128,768]{1,0:T(8,128)(2,1)S(1)} %collective-permute-done.3) | copy-start | bytes 589828
  148.4 11.3 %collective-permute-start.4 = (bf16[128,768]{1,0:T(8,128)(2,1)S(1)}, bf16[128,768]{1,0:T(8,128)(2,1)}, u32[]{:S(2)}, u32[]{:S(2)}) collective-permute-start(bf16[128,768]{1,0:T(8,128)(2,1)S(1)} %collective-permute-done.3), channel_id=1, source_target_pairs={{0,1},{1,2},{2,3},{3,4},{4,5},{5,6},{6,7},{7,8},{8,9},{9,10},{10,1... | collective-permute-start | bytes 589832 | tf_op jit(solution)/shard_map/ppermute | solution.py:22
  154.7 7.0 %copy-start.5 = (f32[128,1152]{0,1:T(8,128)S(1)}, f32[128,1152]{0,1:T(8,128)}, u32[]{:S(2)}) copy-start(f32[128,1152]{0,1:T(8,128)} %copy.54) | copy-start | bytes 1769476
  154.7 7.0 %copy-start.16 = (f32[128,32]{0,1:T(8,128)S(1)}, f32[128,32]{0,1:T(8,128)}, u32[]{:S(2)}) copy-start(f32[128,32]{0,1:T(8,128)} %copy-done.15) | copy-start | bytes 49156
  154.7 7.0 %copy-start.17 = (f32[128,32]{0,1:T(8,128)S(1)}, f32[128,32]{0,1:T(8,128)}, u32[]{:S(2)}) copy-start(f32[128,32]{0,1:T(8,128)} %get-tuple-element.15) | copy-start | bytes 49156
  154.7 18.4 %copy-start.11 = (bf16[128,768]{1,0:T(8,128)(2,1)S(1)}, bf16[128,768]{1,0:T(8,128)(2,1)}, u32[]{:S(2)}) copy-start(bf16[128,768]{1,0:T(8,128)(2,1)} %copy-done.10) | copy-start | bytes 589828
  154.9 40.6 %copy-start.13 = (bf16[128,768]{1,0:T(8,128)(2,1)S(1)}, bf16[128,768]{1,0:T(8,128)(2,1)}, u32[]{:S(2)}) copy-start(bf16[128,768]{1,0:T(8,128)(2,1)} %copy-done.12) | copy-start | bytes 589828
  159.7 11.4 %collective-permute-start.5 = (bf16[128,768]{1,0:T(8,128)(2,1)}, bf16[128,768]{1,0:T(8,128)(2,1)S(1)}, u32[]{:S(2)}, u32[]{:S(2)}) collective-permute-start(bf16[128,768]{1,0:T(8,128)(2,1)} %collective-permute-done.4), channel_id=1, source_target_pairs={{0,1},{1,2},{2,3},{3,4},{4,5},{5,6},{6,7},{7,8},{8,9},{9,10},{10,1... | collective-permute-start | bytes 589832 | tf_op jit(solution)/shard_map/ppermute | solution.py:22
  171.1 11.2 %collective-permute-start.6 = (bf16[128,768]{1,0:T(8,128)(2,1)S(1)}, bf16[128,768]{1,0:T(8,128)(2,1)S(1)}, u32[]{:S(2)}, u32[]{:S(2)}) collective-permute-start(bf16[128,768]{1,0:T(8,128)(2,1)S(1)} %collective-permute-done.5), channel_id=1, source_target_pairs={{0,1},{1,2},{2,3},{3,4},{4,5},{5,6},{6,7},{7,8},{8,9},{9,10},{10,1... | collective-permute-start | bytes 589832 | tf_op jit(solution)/shard_map/ppermute | solution.py:22
  182.3 11.2 %collective-permute-start.7 = (bf16[128,768]{1,0:T(8,128)(2,1)S(1)}, bf16[128,768]{1,0:T(8,128)(2,1)S(1)}, u32[]{:S(2)}, u32[]{:S(2)}) collective-permute-start(bf16[128,768]{1,0:T(8,128)(2,1)S(1)} %collective-permute-done.6), channel_id=1, source_target_pairs={{0,1},{1,2},{2,3},{3,4},{4,5},{5,6},{6,7},{7,8},{8,9},{9,10},{10,1... | collective-permute-start | bytes 589832 | tf_op jit(solution)/shard_map/ppermute | solution.py:22
  193.5 11.2 %collective-permute-start.8 = (bf16[128,768]{1,0:T(8,128)(2,1)S(1)}, bf16[128,768]{1,0:T(8,128)(2,1)S(1)}, u32[]{:S(2)}, u32[]{:S(2)}) collective-permute-start(bf16[128,768]{1,0:T(8,128)(2,1)S(1)} %collective-permute-done.7), channel_id=1, source_target_pairs={{0,1},{1,2},{2,3},{3,4},{4,5},{5,6},{6,7},{7,8},{8,9},{9,10},{10,1... | collective-permute-start | bytes 589832 | tf_op jit(solution)/shard_map/ppermute | solution.py:22
  204.7 11.2 %collective-permute-start.9 = (bf16[128,768]{1,0:T(8,128)(2,1)S(1)}, bf16[128,768]{1,0:T(8,128)(2,1)S(1)}, u32[]{:S(2)}, u32[]{:S(2)}) collective-permute-start(bf16[128,768]{1,0:T(8,128)(2,1)S(1)} %collective-permute-done.8), channel_id=1, source_target_pairs={{0,1},{1,2},{2,3},{3,4},{4,5},{5,6},{6,7},{7,8},{8,9},{9,10},{10,1... | collective-permute-start | bytes 589832 | tf_op jit(solution)/shard_map/ppermute | solution.py:22
  215.9 11.2 %collective-permute-start.10 = (bf16[128,768]{1,0:T(8,128)(2,1)S(1)}, bf16[128,768]{1,0:T(8,128)(2,1)S(1)}, u32[]{:S(2)}, u32[]{:S(2)}) collective-permute-start(bf16[128,768]{1,0:T(8,128)(2,1)S(1)} %collective-permute-done.9), channel_id=1, source_target_pairs={{0,1},{1,2},{2,3},{3,4},{4,5},{5,6},{6,7},{7,8},{8,9},{9,10},{10,1... | collective-permute-start | bytes 589832 | tf_op jit(solution)/shard_map/ppermute | solution.py:22
  227.1 11.2 %collective-permute-start.11 = (bf16[128,768]{1,0:T(8,128)(2,1)S(1)}, bf16[128,768]{1,0:T(8,128)(2,1)S(1)}, u32[]{:S(2)}, u32[]{:S(2)}) collective-permute-start(bf16[128,768]{1,0:T(8,128)(2,1)S(1)} %collective-permute-done.10), channel_id=1, source_target_pairs={{0,1},{1,2},{2,3},{3,4},{4,5},{5,6},{6,7},{7,8},{8,9},{9,10},{10,1... | collective-permute-start | bytes 589832 | tf_op jit(solution)/shard_map/ppermute | solution.py:22
  254.0 8.6 %copy-start.6 = (bf16[1664,384]{0,1:T(8,128)(2,1)S(1)}, bf16[1664,384]{0,1:T(8,128)(2,1)}, u32[]{:S(2)}) copy-start(bf16[1664,384]{0,1:T(8,128)(2,1)} %copy.50) | copy-start | bytes 3833860
  262.7 9.3 %copy-start.14 = (bf16[5,16,1152]{2,1,0:T(8,128)(2,1)S(1)}, bf16[5,16,1152]{2,1,0:T(8,128)(2,1)}, u32[]{:S(2)}) copy-start(bf16[5,16,1152]{2,1,0:T(8,128)(2,1)} %dot_general.51) | copy-start | bytes 552964
  262.7 9.3 %copy-start.28 = (f32[128,5]{0,1:T(8,128)S(1)}, f32[128,5]{0,1:T(8,128)}, u32[]{:S(2)}) copy-start(f32[128,5]{0,1:T(8,128)} %copy-done.27) | copy-start | bytes 7684
  262.7 9.5 %copy-start.9 = (bf16[80,1152]{1,0:T(8,128)(2,1)S(1)}, bf16[80,1152]{1,0:T(8,128)(2,1)}, u32[]{:S(2)}) copy-start(bf16[80,1152]{1,0:T(8,128)(2,1)} %reshape_reshape.9) | copy-start | bytes 552964
  262.7 9.7 %copy-start.4 = (bf16[1152,1152]{1,0:T(8,128)(2,1)S(1)}, bf16[1152,1152]{1,0:T(8,128)(2,1)}, u32[]{:S(2)}) copy-start(bf16[1152,1152]{1,0:T(8,128)(2,1)} %param.21) | copy-start | bytes 7962628
where the time goes:
time: 276 us; the launch traced here: 274 us
  waiting for transfers between devices  118 us (43%)
  local copies, waits for them, and re-layouts  62.1 us (22%)
  starting transfers between devices  31.4 us (11%)
  matrix products  28.8 us (10%)
  other arithmetic  16.9 us (6%)
  blocking collectives  15 us (5%)
    ppermute x12, waiting for transfers between devices, from_behind(): return lax.ppermute(block, axis, route)  92.7 us
    all_to_all x1, waiting for transfers between devices, on_device(): incoming = lax.all_to_all(outgoing, 'tok', 0, 0, tiled=True)  25.3 us
    ppermute x12, starting transfers between devices, from_behind(): return lax.ppermute(block, axis, route)  23.1 us
    all_gather x1, blocking collectives, on_device(): all_slots = lax.all_gather(packed, 'own', axis=0, tiled=True)  15 us
    dot_general x1, matrix products, on_device(): jnp.einsum('iyxv,vip->xiyp', rounded_values, value_head_rows, preferred_e...  9.21 us
    reshape x5, local copies, waits for them, and re-layouts, on_device(): incoming[:, :, col:col + width]  9 us
    dot_general x1, matrix products, on_device(): jnp.einsum('qkzr,ckr->kzqc', query_head_rows, key_head_rows, preferred_el...  8.99 us
    reduce_sum x1, other arithmetic, on_device(): row_total = jnp.sum(exp_scores, axis=-1)  8.61 us
  transfers between devices with their start and end apart: 13, of which 12 were waited for; matrix products, arithmetic and copies ran while one was open for 11% of the time, Pallas kernels for 0%

commit v1 on v0

--- a/solution.py
+++ b/solution.py
@@ -3,6 +3,7 @@
 import jax.numpy as jnp
 from jax import lax
 from jax.sharding import PartitionSpec as P
+from jax.lax import all_to_all, axis_size
 
 D = 1152
 HEADS = 18
@@ -122,7 +123,17 @@
     tables = (qkv_in, q_out, kv_out, o_in, o_out)
     table_shapes = tuple((table.shape[1:] for table in tables))
     packed = jnp.concatenate([table.reshape(per_owner, -1) for table in tables], axis=1)
-    all_slots = lax.all_gather(packed, "own", axis=0, tiled=True)
+
+    def pair_packet_on(x_part, bus_axis):
+        n_parts = axis_size(bus_axis)
+        copies = []
+        for j in range(x_part.ndim):
+            copies.append(n_parts if j == 0 else 1)
+        return all_to_all(
+            jnp.tile(x_part, copies), axis_name=bus_axis, split_axis=0, concat_axis=0, tiled=True
+        )
+
+    all_slots = pair_packet_on(packed, "own")
     own_here = lax.axis_index("own")
     group_blocks = jnp.arange(tok_count, dtype=jnp.int32) * own_count + own_here
     prompt_starts = jnp.cumsum(lengths) - lengths

time: 276 us -> 277 us (level)
  blocking collectives: 15 us -> 0 us
  waiting for transfers between devices: 118 us -> 128 us
  starting transfers between devices: 31.4 us -> 35.7 us
    all_gather x1 -> x0, blocking collectives: 15 us -> none  [on_device(): all_slots = lax.all_gather(packed, 'own', axis=0, tiled=True)]
    all_to_all x0 -> x1, waiting for transfers between devices: none -> 10 us  [pair_packet_on(): all_to_all(jnp.tile(x_part, copies), axis_name=bus_axis, split_axis=0, co...]
    all_to_all x0 -> x1, starting transfers between devices: none -> 4.3 us  [pair_packet_on(): all_to_all(jnp.tile(x_part, copies), axis_name=bus_axis, split_axis=0, co...]
  transfers between devices with their start and end apart: 13 -> 14, of which waited for: 12 -> 13; matrix products, arithmetic and copies ran while one was open for 11% -> 13% of each run, Pallas kernels for 0% -> 0%
where the time goes in v1:
time: 277 us; the launch traced here: 275 us
  waiting for transfers between devices  128 us (46%)
  local copies, waits for them, and re-layouts  64.6 us (23%)
  starting transfers between devices  35.7 us (13%)
  matrix products  28.8 us (10%)
  other arithmetic  16.2 us (6%)
    ppermute x12, waiting for transfers between devices, from_behind(): return lax.ppermute(block, axis, route)  92.9 us
    all_to_all x1, waiting for transfers between devices, on_device(): incoming = lax.all_to_all(outgoing, 'tok', 0, 0, tiled=True)  25.1 us
    ppermute x12, starting transfers between devices, from_behind(): return lax.ppermute(block, axis, route)  23.1 us
    all_to_all x1, waiting for transfers between devices, pair_packet_on(): all_to_all(jnp.tile(x_part, copies), axis_name=bus_axis, split_axis=0, co...  10 us
    dot_general x1, matrix products, on_device(): jnp.einsum('iyxv,vip->xiyp', rounded_values, value_head_rows, preferred_e...  9.21 us
    reshape x5, local copies, waits for them, and re-layouts, on_device(): incoming[:, :, col:col + width]  9 us
    dot_general x1, matrix products, on_device(): jnp.einsum('qkzr,ckr->kzqc', query_head_rows, key_head_rows, preferred_el...  8.99 us
    reduce_sum x1, other arithmetic, on_device(): row_total = jnp.sum(exp_scores, axis=-1)  8.61 us
  transfers between devices with their start and end apart: 14, of which 13 were waited for; matrix products, arithmetic and copies ran while one was open for 13% of the time, Pallas kernels for 0%

profile of v1, /device:TPU:24, one launch (start us, length us, event | category | flops | bytes accessed | tf_op | source)
XLA Modules:
  0.0 274.9 jit_solution(5658722360890389971)
XLA Ops:
  6.6 4.3 %all-to-all-start = ((bf16[8,8,7680]{2,1,0:T(8,128)(2,1)}), bf16[8,8,7680]{2,1,0:T(8,128)(2,1)}, u32[]{:S(2)}, u32[]{:S(2)}) async-start(bf16[8,8,7680]{2,1,0:T(8,128)(2,1)} %tile.2), calls=%async_computation | async-start | bytes 1966080 | tf_op jit(solution)/shard_map/all_to_all | solution.py:132
  16.2 10.0 %all-to-all-done = bf16[8,8,7680]{2,1,0:T(8,128)(2,1)} async-done(((bf16[8,8,7680]{2,1,0:T(8,128)(2,1)}), bf16[8,8,7680]{2,1,0:T(8,128)(2,1)}, u32[]{:S(2)}, u32[]{:S(2)}) %all-to-all-start) | async-done | bytes 983072 | tf_op jit(solution)/shard_map/all_to_all | solution.py:132
  26.2 4.8 %gather_fusion = bf16[80,7680]{1,0:T(8,128)(2,1)} fusion(bf16[64,7680]{1,0:T(8,128)(2,1)} %bitcast.2, s32[1024]{0:T(1024)S(1)} %pad_clamp_fusion), kind=kCustom, calls=%fused_computation.2 | custom fusion | bytes 2457920 | tf_op jit(solution)/shard_map/jit(_take)/gather | solution.py:150
  31.1 2.6 gather.10
  33.7 3.1 %broadcast_select_fusion = bf16[16,5,7680]{2,1,0:T(8,128)(2,1)} fusion(bf16[16,5,7680]{2,1,0:T(8,128)(2,1)} %gather.10, pred[16,5]{1,0:T(8,128)(4,1)S(1)} %get-tuple-element.3), kind=kLoop, calls=%fused_computation.18 | loop fusion | flops 614400 | bytes 2457680 | tf_op jit(solution)/shard_map/jit(_take)/select_n | solution.py:150
  36.8 8.3 %all-to-all-start.1 = ((bf16[16,5,7680]{2,1,0:T(8,128)(2,1)}), bf16[16,5,7680]{2,1,0:T(8,128)(2,1)}, u32[]{:S(2)}, u32[]{:S(2)}) async-start(bf16[16,5,7680]{2,1,0:T(8,128)(2,1)} %broadcast_select_fusion), calls=%async_computation.1 | async-start | bytes 3932160 | tf_op jit(solution)/shard_map/all_to_all | solution.py:153
  46.0 25.1 %all-to-all-done.1 = bf16[16,5,7680]{2,1,0:T(8,128)(2,1)} async-done(((bf16[16,5,7680]{2,1,0:T(8,128)(2,1)}), bf16[16,5,7680]{2,1,0:T(8,128)(2,1)}, u32[]{:S(2)}, u32[]{:S(2)}) %all-to-all-start.1) | async-done | bytes 1228832 | tf_op jit(solution)/shard_map/all_to_all | solution.py:153
  72.1 1.9 reshape.341
  73.9 2.2 copy.46
  76.1 2.3 reshape.342
  79.8 2.7 reshape.340
  82.5 2.4 copy.44
  84.9 2.2 dot_general.41
  93.9 1.9 collective-permute-start
  95.9 9.3 %collective-permute-done = bf16[128,768]{1,0:T(8,128)(2,1)S(1)} collective-permute-done((bf16[128,768]{1,0:T(8,128)(2,1)S(1)}, bf16[128,768]{1,0:T(8,128)(2,1)S(1)}, u32[]{:S(2)}, u32[]{:S(2)}) %collective-permute-start) | collective-permute-done | bytes 196640 | tf_op jit(solution)/shard_map/ppermute | solution.py:23
  105.1 1.9 collective-permute-start.1
  108.1 8.3 %collective-permute-done.1 = bf16[128,768]{1,0:T(8,128)(2,1)} collective-permute-done((bf16[128,768]{1,0:T(8,128)(2,1)S(1)}, bf16[128,768]{1,0:T(8,128)(2,1)}, u32[]{:S(2)}, u32[]{:S(2)}) %collective-permute-start.1) | collective-permute-done | bytes 196640 | tf_op jit(solution)/shard_map/ppermute | solution.py:23
  116.4 2.1 collective-permute-start.2
  118.5 2.0 fusion.43
  124.9 2.0 reshape_reshape.9
  126.9 1.7 copy.55
  130.8 2.0 dot_general.51
  138.1 1.9 collective-permute-start.3
  141.0 8.5 %collective-permute-done.3 = bf16[128,768]{1,0:T(8,128)(2,1)S(1)} collective-permute-done((bf16[128,768]{1,0:T(8,128)(2,1)}, bf16[128,768]{1,0:T(8,128)(2,1)S(1)}, u32[]{:S(2)}, u32[]{:S(2)}) %collective-permute-start.3) | collective-permute-done | bytes 196640 | tf_op jit(solution)/shard_map/ppermute | solution.py:23
  149.5 1.9 collective-permute-start.4
  151.4 2.2 convolution_add_fusion.1
  153.6 2.1 copy.53
  156.0 4.8 %collective-permute-done.4 = bf16[128,768]{1,0:T(8,128)(2,1)} collective-permute-done((bf16[128,768]{1,0:T(8,128)(2,1)S(1)}, bf16[128,768]{1,0:T(8,128)(2,1)}, u32[]{:S(2)}, u32[]{:S(2)}) %collective-permute-start.4) | collective-permute-done | bytes 196640 | tf_op jit(solution)/shard_map/ppermute | solution.py:23
  160.8 1.9 collective-permute-start.5
  162.9 9.4 %collective-permute-done.5 = bf16[128,768]{1,0:T(8,128)(2,1)S(1)} collective-permute-done((bf16[128,768]{1,0:T(8,128)(2,1)}, bf16[128,768]{1,0:T(8,128)(2,1)S(1)}, u32[]{:S(2)}, u32[]{:S(2)}) %collective-permute-start.5) | collective-permute-done | bytes 196640 | tf_op jit(solution)/shard_map/ppermute | solution.py:23
  172.2 1.9 collective-permute-start.6
  174.2 9.2 %collective-permute-done.6 = bf16[128,768]{1,0:T(8,128)(2,1)S(1)} collective-permute-done((bf16[128,768]{1,0:T(8,128)(2,1)S(1)}, bf16[128,768]{1,0:T(8,128)(2,1)S(1)}, u32[]{:S(2)}, u32[]{:S(2)}) %collective-permute-start.6) | collective-permute-done | bytes 196640 | tf_op jit(solution)/shard_map/ppermute | solution.py:23
  183.4 1.9 collective-permute-start.7
  187.2 7.4 %collective-permute-done.7 = bf16[128,768]{1,0:T(8,128)(2,1)S(1)} collective-permute-done((bf16[128,768]{1,0:T(8,128)(2,1)S(1)}, bf16[128,768]{1,0:T(8,128)(2,1)S(1)}, u32[]{:S(2)}, u32[]{:S(2)}) %collective-permute-start.7) | collective-permute-done | bytes 196640 | tf_op jit(solution)/shard_map/ppermute | solution.py:23
  194.6 1.9 collective-permute-start.8
  197.5 8.3 %collective-permute-done.8 = bf16[128,768]{1,0:T(8,128)(2,1)S(1)} collective-permute-done((bf16[128,768]{1,0:T(8,128)(2,1)S(1)}, bf16[128,768]{1,0:T(8,128)(2,1)S(1)}, u32[]{:S(2)}, u32[]{:S(2)}) %collective-permute-start.8) | collective-permute-done | bytes 196640 | tf_op jit(solution)/shard_map/ppermute | solution.py:23
  205.8 1.9 collective-permute-start.9
  207.8 9.2 %collective-permute-done.9 = bf16[128,768]{1,0:T(8,128)(2,1)S(1)} collective-permute-done((bf16[128,768]{1,0:T(8,128)(2,1)S(1)}, bf16[128,768]{1,0:T(8,128)(2,1)S(1)}, u32[]{:S(2)}, u32[]{:S(2)}) %collective-permute-start.9) | collective-permute-done | bytes 196640 | tf_op jit(solution)/shard_map/ppermute | solution.py:23
  217.0 1.9 collective-permute-start.10
  219.0 9.2 %collective-permute-done.10 = bf16[128,768]{1,0:T(8,128)(2,1)S(1)} collective-permute-done((bf16[128,768]{1,0:T(8,128)(2,1)S(1)}, bf16[128,768]{1,0:T(8,128)(2,1)S(1)}, u32[]{:S(2)}, u32[]{:S(2)}) %collective-permute-start.10) | collective-permute-done | bytes 196640 | tf_op jit(solution)/shard_map/ppermute | solution.py:23
  228.2 1.9 collective-permute-start.11
  230.2 9.2 %collective-permute-done.11 = bf16[128,768]{1,0:T(8,128)(2,1)S(1)} collective-permute-done((bf16[128,768]{1,0:T(8,128)(2,1)S(1)}, bf16[128,768]{1,0:T(8,128)(2,1)S(1)}, u32[]{:S(2)}, u32[]{:S(2)}) %collective-permute-start.11) | collective-permute-done | bytes 196640 | tf_op jit(solution)/shard_map/ppermute | solution.py:23
  239.4 1.8 fusion.42
  241.2 2.5 copy.50
  243.7 2.5 copy.49
  246.2 9.0 %fusion.2 = (f32[6,3,128]{2,1,0:T(4,128)S(1)}, f32[6,1664,128,3]{2,1,3,0:T(8,128)}) fusion(pred[128,1664]{0,1:T(8,128)(4,1)S(1)} %compare_and_fusion, bf16[1664,6,64,1]{0,2,3,1:T(8,128)(2,1)} %bitcast.102, bf16[128,6,3,64]{0,3,2,1:T(8,128)(2,1)S(1)} %bitcast.106), kind=kOutput, calls=%fused_computation.7 | convolution fusion | flops 502232832 | bytes 17130496 | tf_op jit(solution)/shard_map/qkzr,ckr->kzqc/dot_general | solution.py:206
  255.2 8.6 %fusion = f32[6,3,128]{2,1,0:T(4,128)S(1)} fusion(f32[6,1664,128,3]{2,1,3,0:T(8,128)} %get-tuple-element.17, f32[6,3,128]{2,1,0:T(4,128)S(1)} %get-tuple-element.16, pred[128,1664]{0,1:T(8,128)(4,1)S(1)} %compare_and_fusion), kind=kLoop, calls=%fused_computation.5 | loop fusion | flops 15333120 | bytes 15566848 | tf_op jit(solution)/shard_map/reduce_sum | solution.py:212
  263.9 9.2 %fusion.23 = bf16[128,6,3,64]{0,3,2,1:T(8,128)(2,1)S(1)} fusion(bf16[1664,6,64,1]{0,2,3,1:T(8,128)(2,1)S(1)} %bitcast.110, f32[6,1664,128,3]{2,1,3,0:T(8,128)} %get-tuple-element.17, f32[6,3,128]{2,1,0:T(4,128)S(1)} %get-tuple-element.16, pred[128,1664]{0,1:T(8,128)(4,1)S(1)} %compare_and_fusion, f32[128,6,3]{0,2,1:T(4,128)S(1)} %bitcast.117), kind=kOutput, calls=%fused_computation.34 | convolution fusion | flops 506363904 | bytes 17139712 | tf_op jit(solution)/shard_map/iyxv,vip->xiyp/dot_general | solution.py:214
  (157 shorter events, 39.8 us)
Async XLA Ops:
  0.6 150.8 %copy-start = (bf16[1152,1152]{1,0:T(8,128)(2,1)S(1)}, bf16[1152,1152]{1,0:T(8,128)(2,1)}, u32[]{:S(2)}) copy-start(bf16[1152,1152]{1,0:T(8,128)(2,1)} %param.18) | copy-start | bytes 7962628
  0.6 10.3 %copy-start.27 = (s32[64]{0:T(128)S(1)}, s32[64]{0:T(128)}, u32[]{:S(2)}) copy-start(s32[64]{0:T(128)} %param.27) | copy-start | bytes 772
  0.7 11.0 %copy-start.1 = (s32[64]{0:T(128)S(1)}, s32[64]{0:T(128)}, u32[]{:S(2)}) copy-start(s32[64]{0:T(128)} %param.28) | copy-start | bytes 772
  6.6 19.6 %all-to-all-start = ((bf16[8,8,7680]{2,1,0:T(8,128)(2,1)}), bf16[8,8,7680]{2,1,0:T(8,128)(2,1)}, u32[]{:S(2)}, u32[]{:S(2)}) async-start(bf16[8,8,7680]{2,1,0:T(8,128)(2,1)} %tile.2), calls=%async_computation | async-start | bytes 1966080 | tf_op jit(solution)/shard_map/all_to_all | solution.py:132
  11.6 1.5 copy-start.2
  13.2 2.9 %copy-start.3 = (bf16[128,1152]{1,0:T(8,128)(2,1)S(1)}, bf16[128,1152]{1,0:T(8,128)(2,1)}, u32[]{:S(2)}) copy-start(bf16[128,1152]{1,0:T(8,128)(2,1)} %param.16) | copy-start | bytes 884740
  14.7 16.3 %copy-start.28 = (s32[128]{0:T(128)}, s32[128]{0:T(128)S(1)}, u32[]{:S(2)}) copy-start(s32[128]{0:T(128)S(1)} %iota_add_fusion.1) | copy-start | bytes 1540
  14.7 0.6 copy-start.19
  14.9 30.3 %copy-start.30 = (s32[128]{0:T(128)}, s32[128]{0:T(128)S(1)}, u32[]{:S(2)}) copy-start(s32[128]{0:T(128)S(1)} %broadcast_add_fusion.1) | copy-start | bytes 1540
  36.8 8.3 %copy-start.24 = (bf16[1152]{0:T(1024)(128)(2,1)S(1)}, bf16[1152]{0:T(1024)(128)(2,1)}, u32[]{:S(2)}) copy-start(bf16[1152]{0:T(1024)(128)(2,1)} %param.17) | copy-start | bytes 6916
  36.8 34.3 %all-to-all-start.1 = ((bf16[16,5,7680]{2,1,0:T(8,128)(2,1)}), bf16[16,5,7680]{2,1,0:T(8,128)(2,1)}, u32[]{:S(2)}, u32[]{:S(2)}) async-start(bf16[16,5,7680]{2,1,0:T(8,128)(2,1)} %broadcast_select_fusion), calls=%async_computation.1 | async-start | bytes 3932160 | tf_op jit(solution)/shard_map/all_to_all | solution.py:153
  45.2 41.9 %copy-start.18 = (f32[1152]{0:T(1024)}, f32[1152]{0:T(1024)S(1)}, u32[]{:S(2)}) copy-start(f32[1152]{0:T(1024)S(1)} %convert_element_type.91) | copy-start | bytes 13828
  45.2 41.9 %copy-start.23 = (f32[128]{0:T(128)}, f32[128]{0:T(128)S(1)}, u32[]{:S(2)}) copy-start(f32[128]{0:T(128)S(1)} %add_rsqrt_fusion) | copy-start | bytes 1540
  45.3 41.8 %copy-start.25 = (f32[128,5]{0,1:T(8,128)}, f32[128,5]{0,1:T(8,128)S(1)}, u32[]{:S(2)}) copy-start(f32[128,5]{0,1:T(8,128)S(1)} %fusion.34) | copy-start | bytes 7684
  46.0 45.4 %copy-start.15 = (f32[128,32]{0,1:T(8,128)}, f32[128,32]{0,1:T(8,128)S(1)}, u32[]{:S(2)}) copy-start(f32[128,32]{0,1:T(8,128)S(1)} %get-tuple-element.14) | copy-start | bytes 49156
  87.5 2.1 copy-start.21
  91.4 4.5 %copy-start.22 = (s32[1664]{0:T(1024)S(1)}, s32[1664]{0:T(1024)}, u32[]{:S(2)}) copy-start(s32[1664]{0:T(1024)} %convert_reduce_fusion) | copy-start | bytes 19972
  91.4 15.7 %copy-start.20 = (s32[1664]{0:T(1024)S(1)}, s32[1664]{0:T(1024)}, u32[]{:S(2)}) copy-start(s32[1664]{0:T(1024)} %copy-done.19) | copy-start | bytes 19972
  91.4 15.7 %copy-start.29 = (s32[128]{0:T(128)S(1)}, s32[128]{0:T(128)}, u32[]{:S(2)}) copy-start(s32[128]{0:T(128)} %copy-done.28) | copy-start | bytes 1540
  91.4 15.7 %copy-start.31 = (s32[128]{0:T(128)S(1)}, s32[128]{0:T(128)}, u32[]{:S(2)}) copy-start(s32[128]{0:T(128)} %copy-done.30) | copy-start | bytes 1540
  93.9 22.5 %copy-start.7 = (bf16[128,768]{1,0:T(8,128)(2,1)}, bf16[128,768]{1,0:T(8,128)(2,1)S(1)}, u32[]{:S(2)}) copy-start(bf16[128,768]{1,0:T(8,128)(2,1)S(1)} %pad_maximum_fusion.1) | copy-start | bytes 589828
  93.9 11.2 %collective-permute-start = (bf16[128,768]{1,0:T(8,128)(2,1)S(1)}, bf16[128,768]{1,0:T(8,128)(2,1)S(1)}, u32[]{:S(2)}, u32[]{:S(2)}) collective-permute-start(bf16[128,768]{1,0:T(8,128)(2,1)S(1)} %pad_maximum_fusion.1), channel_id=1, source_target_pairs={{0,1},{1,2},{2,3},{3,4},{4,5},{5,6},{6,7},{7,8},{8,9},{9,10},{10,1... | collective-permute-start | bytes 589832 | tf_op jit(solution)/shard_map/ppermute | solution.py:23
  105.1 11.3 %copy-start.10 = (bf16[128,768]{1,0:T(8,128)(2,1)}, bf16[128,768]{1,0:T(8,128)(2,1)S(1)}, u32[]{:S(2)}) copy-start(bf16[128,768]{1,0:T(8,128)(2,1)S(1)} %collective-permute-done) | copy-start | bytes 589828
  105.1 11.3 %collective-permute-start.1 = (bf16[128,768]{1,0:T(8,128)(2,1)S(1)}, bf16[128,768]{1,0:T(8,128)(2,1)}, u32[]{:S(2)}, u32[]{:S(2)}) collective-permute-start(bf16[128,768]{1,0:T(8,128)(2,1)S(1)} %collective-permute-done), channel_id=1, source_target_pairs={{0,1},{1,2},{2,3},{3,4},{4,5},{5,6},{6,7},{7,8},{8,9},{9,10},{10,1... | collective-permute-start | bytes 589832 | tf_op jit(solution)/shard_map/ppermute | solution.py:23
  116.4 21.6 %collective-permute-start.2 = (bf16[128,768]{1,0:T(8,128)(2,1)}, bf16[128,768]{1,0:T(8,128)(2,1)}, u32[]{:S(2)}, u32[]{:S(2)}) collective-permute-start(bf16[128,768]{1,0:T(8,128)(2,1)} %collective-permute-done.1), channel_id=1, source_target_pairs={{0,1},{1,2},{2,3},{3,4},{4,5},{5,6},{6,7},{7,8},{8,9},{9,10},{10,1... | collective-permute-start | bytes 589832 | tf_op jit(solution)/shard_map/ppermute | solution.py:23
  138.1 11.4 %collective-permute-start.3 = (bf16[128,768]{1,0:T(8,128)(2,1)}, bf16[128,768]{1,0:T(8,128)(2,1)S(1)}, u32[]{:S(2)}, u32[]{:S(2)}) collective-permute-start(bf16[128,768]{1,0:T(8,128)(2,1)} %collective-permute-done.2), channel_id=1, source_target_pairs={{0,1},{1,2},{2,3},{3,4},{4,5},{5,6},{6,7},{7,8},{8,9},{9,10},{10,1... | collective-permute-start | bytes 589832 | tf_op jit(solution)/shard_map/ppermute | solution.py:23
  141.0 14.8 %copy-start.8 = (bf16[128,768]{1,0:T(8,128)(2,1)S(1)}, bf16[128,768]{1,0:T(8,128)(2,1)}, u32[]{:S(2)}) copy-start(bf16[128,768]{1,0:T(8,128)(2,1)} %copy-done.7) | copy-start | bytes 589828
  149.5 6.2 %copy-start.12 = (bf16[128,768]{1,0:T(8,128)(2,1)}, bf16[128,768]{1,0:T(8,128)(2,1)S(1)}, u32[]{:S(2)}) copy-start(bf16[128,768]{1,0:T(8,128)(2,1)S(1)} %collective-permute-done.3) | copy-start | bytes 589828
  149.5 11.3 %collective-permute-start.4 = (bf16[128,768]{1,0:T(8,128)(2,1)S(1)}, bf16[128,768]{1,0:T(8,128)(2,1)}, u32[]{:S(2)}, u32[]{:S(2)}) collective-permute-start(bf16[128,768]{1,0:T(8,128)(2,1)S(1)} %collective-permute-done.3), channel_id=1, source_target_pairs={{0,1},{1,2},{2,3},{3,4},{4,5},{5,6},{6,7},{7,8},{8,9},{9,10},{10,1... | collective-permute-start | bytes 589832 | tf_op jit(solution)/shard_map/ppermute | solution.py:23
  155.8 7.0 %copy-start.5 = (f32[128,1152]{0,1:T(8,128)S(1)}, f32[128,1152]{0,1:T(8,128)}, u32[]{:S(2)}) copy-start(f32[128,1152]{0,1:T(8,128)} %copy.53) | copy-start | bytes 1769476
  155.8 7.0 %copy-start.16 = (f32[128,32]{0,1:T(8,128)S(1)}, f32[128,32]{0,1:T(8,128)}, u32[]{:S(2)}) copy-start(f32[128,32]{0,1:T(8,128)} %copy-done.15) | copy-start | bytes 49156
  155.8 7.0 %copy-start.17 = (f32[128,32]{0,1:T(8,128)S(1)}, f32[128,32]{0,1:T(8,128)}, u32[]{:S(2)}) copy-start(f32[128,32]{0,1:T(8,128)} %get-tuple-element.15) | copy-start | bytes 49156
  155.8 18.4 %copy-start.11 = (bf16[128,768]{1,0:T(8,128)(2,1)S(1)}, bf16[128,768]{1,0:T(8,128)(2,1)}, u32[]{:S(2)}) copy-start(bf16[128,768]{1,0:T(8,128)(2,1)} %copy-done.10) | copy-start | bytes 589828
  156.0 40.6 %copy-start.13 = (bf16[128,768]{1,0:T(8,128)(2,1)S(1)}, bf16[128,768]{1,0:T(8,128)(2,1)}, u32[]{:S(2)}) copy-start(bf16[128,768]{1,0:T(8,128)(2,1)} %copy-done.12) | copy-start | bytes 589828
  160.8 11.4 %collective-permute-start.5 = (bf16[128,768]{1,0:T(8,128)(2,1)}, bf16[128,768]{1,0:T(8,128)(2,1)S(1)}, u32[]{:S(2)}, u32[]{:S(2)}) collective-permute-start(bf16[128,768]{1,0:T(8,128)(2,1)} %collective-permute-done.4), channel_id=1, source_target_pairs={{0,1},{1,2},{2,3},{3,4},{4,5},{5,6},{6,7},{7,8},{8,9},{9,10},{10,1... | collective-permute-start | bytes 589832 | tf_op jit(solution)/shard_map/ppermute | solution.py:23
  172.2 11.2 %collective-permute-start.6 = (bf16[128,768]{1,0:T(8,128)(2,1)S(1)}, bf16[128,768]{1,0:T(8,128)(2,1)S(1)}, u32[]{:S(2)}, u32[]{:S(2)}) collective-permute-start(bf16[128,768]{1,0:T(8,128)(2,1)S(1)} %collective-permute-done.5), channel_id=1, source_target_pairs={{0,1},{1,2},{2,3},{3,4},{4,5},{5,6},{6,7},{7,8},{8,9},{9,10},{10,1... | collective-permute-start | bytes 589832 | tf_op jit(solution)/shard_map/ppermute | solution.py:23
  183.4 11.2 %collective-permute-start.7 = (bf16[128,768]{1,0:T(8,128)(2,1)S(1)}, bf16[128,768]{1,0:T(8,128)(2,1)S(1)}, u32[]{:S(2)}, u32[]{:S(2)}) collective-permute-start(bf16[128,768]{1,0:T(8,128)(2,1)S(1)} %collective-permute-done.6), channel_id=1, source_target_pairs={{0,1},{1,2},{2,3},{3,4},{4,5},{5,6},{6,7},{7,8},{8,9},{9,10},{10,1... | collective-permute-start | bytes 589832 | tf_op jit(solution)/shard_map/ppermute | solution.py:23
  194.6 11.2 %collective-permute-start.8 = (bf16[128,768]{1,0:T(8,128)(2,1)S(1)}, bf16[128,768]{1,0:T(8,128)(2,1)S(1)}, u32[]{:S(2)}, u32[]{:S(2)}) collective-permute-start(bf16[128,768]{1,0:T(8,128)(2,1)S(1)} %collective-permute-done.7), channel_id=1, source_target_pairs={{0,1},{1,2},{2,3},{3,4},{4,5},{5,6},{6,7},{7,8},{8,9},{9,10},{10,1... | collective-permute-start | bytes 589832 | tf_op jit(solution)/shard_map/ppermute | solution.py:23
  205.8 11.2 %collective-permute-start.9 = (bf16[128,768]{1,0:T(8,128)(2,1)S(1)}, bf16[128,768]{1,0:T(8,128)(2,1)S(1)}, u32[]{:S(2)}, u32[]{:S(2)}) collective-permute-start(bf16[128,768]{1,0:T(8,128)(2,1)S(1)} %collective-permute-done.8), channel_id=1, source_target_pairs={{0,1},{1,2},{2,3},{3,4},{4,5},{5,6},{6,7},{7,8},{8,9},{9,10},{10,1... | collective-permute-start | bytes 589832 | tf_op jit(solution)/shard_map/ppermute | solution.py:23
  217.0 11.2 %collective-permute-start.10 = (bf16[128,768]{1,0:T(8,128)(2,1)S(1)}, bf16[128,768]{1,0:T(8,128)(2,1)S(1)}, u32[]{:S(2)}, u32[]{:S(2)}) collective-permute-start(bf16[128,768]{1,0:T(8,128)(2,1)S(1)} %collective-permute-done.9), channel_id=1, source_target_pairs={{0,1},{1,2},{2,3},{3,4},{4,5},{5,6},{6,7},{7,8},{8,9},{9,10},{10,1... | collective-permute-start | bytes 589832 | tf_op jit(solution)/shard_map/ppermute | solution.py:23
  228.2 11.2 %collective-permute-start.11 = (bf16[128,768]{1,0:T(8,128)(2,1)S(1)}, bf16[128,768]{1,0:T(8,128)(2,1)S(1)}, u32[]{:S(2)}, u32[]{:S(2)}) collective-permute-start(bf16[128,768]{1,0:T(8,128)(2,1)S(1)} %collective-permute-done.10), channel_id=1, source_target_pairs={{0,1},{1,2},{2,3},{3,4},{4,5},{5,6},{6,7},{7,8},{8,9},{9,10},{10,1... | collective-permute-start | bytes 589832 | tf_op jit(solution)/shard_map/ppermute | solution.py:23
  255.2 8.6 %copy-start.6 = (bf16[1664,384]{0,1:T(8,128)(2,1)S(1)}, bf16[1664,384]{0,1:T(8,128)(2,1)}, u32[]{:S(2)}) copy-start(bf16[1664,384]{0,1:T(8,128)(2,1)} %copy.49) | copy-start | bytes 3833860
  263.8 9.3 %copy-start.14 = (bf16[5,16,1152]{2,1,0:T(8,128)(2,1)S(1)}, bf16[5,16,1152]{2,1,0:T(8,128)(2,1)}, u32[]{:S(2)}) copy-start(bf16[5,16,1152]{2,1,0:T(8,128)(2,1)} %dot_general.51) | copy-start | bytes 552964
  263.8 9.3 %copy-start.26 = (f32[128,5]{0,1:T(8,128)S(1)}, f32[128,5]{0,1:T(8,128)}, u32[]{:S(2)}) copy-start(f32[128,5]{0,1:T(8,128)} %copy-done.25) | copy-start | bytes 7684
  263.9 9.5 %copy-start.9 = (bf16[80,1152]{1,0:T(8,128)(2,1)S(1)}, bf16[80,1152]{1,0:T(8,128)(2,1)}, u32[]{:S(2)}) copy-start(bf16[80,1152]{1,0:T(8,128)(2,1)} %reshape_reshape.9) | copy-start | bytes 552964
  263.9 9.7 %copy-start.4 = (bf16[1152,1152]{1,0:T(8,128)(2,1)S(1)}, bf16[1152,1152]{1,0:T(8,128)(2,1)}, u32[]{:S(2)}) copy-start(bf16[1152,1152]{1,0:T(8,128)(2,1)} %param.21) | copy-start | bytes 7962628
